TPU v7x, 256 devices: a whole 4x4x8 slice. The times are simulated.
256 devices in a mesh: dp: 4 (over y), seq: 16 (over z, core), tensor: 4 (over x).
Axes of the slice: x: 4, y: 4, z: 8, core: 2. Of those that a mesh axis runs over, the one named last changes fastest.
Arguments:
- queries: bfloat16 [16384, 8192], P(('dp', 'seq'), 'tensor'), parts along dimension 0, may hold values from -110 to 110
- keys_values: bfloat16 [16384, 2, 1024], P(('dp', 'seq'), None, 'tensor'), parts along dimension 0, may hold values from -4.5 to 4.5
- out_weight: bfloat16 [8192, 8192], P('tensor', 'seq'), may hold values from -0.1875 to 0.1875
- residual: bfloat16 [16384, 8192], P(('dp', 'tensor'), 'seq'), parts along dimension 0, may hold values from -3 to 3
- segments: int32 [16384], P('dp'), parts along dimension 0, may hold values from 0 to 3, never falling along the last dimension, each value on 1 to 2048 neighbouring positions
Outputs:
- layer_out: bfloat16 [16384, 8192], P(('dp', 'tensor'), 'seq'), parts along dimension 0
There are 4 independent parts, one for each index of `dp`. A program takes and returns all parts, laid end to end along the dimension named above; an argument that names none is the same for every part. Nothing has to cross between parts.
Inputs may be any that keep to these rules, and one draw needn't show every extreme that they name: `segments`: segment numbers never fall along the tokens.
All inputs are finite; a program needn't handle non-finite values.
Results may differ from a plain program's by a relative error of at most 0.0085.
Values may be sent and summed in bfloat16 or wider, within the bound.
No kernel may reach another device: no remote copies, remote signals or barrier semaphores. Data moves between devices by JAX's collectives and lax.ppermute only.
A program may use at most 128 MiB of HBM per device.

v0:
```python
import jax
import jax.numpy as jnp
import numpy as np
from jax import lax
from jax.sharding import PartitionSpec as P

H = 64
KVH = 8
HD = 128
L = 4096
CHUNKS = 4


def attend_rows(query_head, key_head, value_head, doc_ids, first_row, rows):
    key_end = first_row + rows
    query_block = query_head[first_row:key_end]
    raw_scores = jnp.einsum(
        "qd,kd->qk", query_block, key_head[:key_end], preferred_element_type=jnp.float32
    ) * HD ** (-0.5)
    query_pos = first_row + jnp.arange(rows)[:, None]
    key_pos = jnp.arange(key_end)[None, :]
    same_doc = doc_ids[first_row:key_end, None] == doc_ids[None, :key_end]
    allowed = (key_pos <= query_pos) & same_doc
    masked = jnp.where(allowed, raw_scores, -1e30)
    highest = jnp.max(masked, axis=-1, keepdims=True)
    exponents = jnp.where(allowed, jnp.exp(masked - highest), 0.0)
    weights = (exponents / jnp.sum(exponents, axis=-1, keepdims=True)).astype(jnp.bfloat16)
    blended = jnp.einsum(
        "qk,kd->qd", weights, value_head[:key_end], preferred_element_type=jnp.float32
    )
    return blended.astype(jnp.bfloat16)


def on_device(queries, keys_values, out_weight, residual, segments):
    n_seq = lax.axis_size("seq")
    n_ten = lax.axis_size("tensor")
    seq_idx = lax.axis_index("seq")
    tok_dev = queries.shape[0]
    heads_ten = queries.shape[1] // HD
    heads_dev = heads_ten // n_seq
    assert heads_dev == 1
    group_size = H // KVH
    query_slab = queries.reshape(tok_dev, 1, heads_ten * HD)
    query_all = lax.all_to_all(query_slab, "seq", split_axis=2, concat_axis=0, tiled=True)
    query_head = query_all.reshape(query_all.shape[0], HD)
    rows_all = query_head.shape[0]
    assert rows_all == L
    pair_all = lax.all_gather(keys_values, "seq", axis=0, tiled=True)
    kv_local = seq_idx // group_size
    pair_head = lax.dynamic_slice_in_dim(pair_all, kv_local * HD, HD, axis=2)
    key_head = pair_head[:, 0, :]
    value_head = pair_head[:, 1, :]
    doc_ids = segments
    out_rows = rows_all // n_ten
    block_rows = out_rows // CHUNKS
    pieces = []
    for chunk in range(CHUNKS):
        blocks = [
            attend_rows(
                query_head,
                key_head,
                value_head,
                doc_ids,
                part * out_rows + chunk * block_rows,
                block_rows,
            )
            for part in range(n_ten)
        ]
        chunk_heads = jnp.concatenate(blocks, axis=0)
        gathered = lax.all_gather(chunk_heads, "seq", axis=1, tiled=True)
        projected = jnp.dot(gathered, out_weight, preferred_element_type=jnp.float32)
        pieces.append(lax.psum_scatter(projected, "tensor", scatter_dimension=0, tiled=True))
    summed = jnp.concatenate(pieces, axis=0)
    return (residual.astype(jnp.float32) + summed).astype(jnp.bfloat16)


def solution(mesh):
    placed = (
        P(("dp", "seq"), "tensor"),
        P(("dp", "seq"), None, "tensor"),
        P("tensor", "seq"),
        P(("dp", "tensor"), "seq"),
        P("dp"),
    )
    return jax.shard_map(
        on_device, mesh=mesh, in_specs=placed, out_specs=P(("dp", "tensor"), "seq"), check_vma=False
    )
```

profile of v0, /device:TPU:1, one launch (start us, length us, event | category | flops | bytes accessed | tf_op | source)
XLA Modules:
  0.0 436.0 jit_solution(1249033622516324133)
XLA Ops:
  6.5 1.8 copy.43
  8.4 5.9 %copy.44 = bf16[256,1,2048]{0,1,2:T(2,128)(2,1)} copy(bf16[256,1,2048]{2,0,1:T(8,128)(2,1)} %bitcast.316) | data formatting | bytes 2097152 | tf_op jit(solution)/shard_map/reshape | solution.py:43
  14.8 11.6 %reduce = bf16[2048,256]{1,0:T(8,128)(2,1)S(1)} reduce(bf16[2048,1,256]{2,1,0:T(2,128)(2,1)} %bitcast.306, bf16[]{:T(256)} %broadcast.172), dimensions={1}, to_apply=%bitcast.228.reduce_sub_computation | reduce | bytes 2097154
  26.5 1.1 reshape.191
  27.6 10.0 %all-to-all-start = ((bf16[16,2,16384]{2,1,0:T(2,128)(2,1)}), bf16[16,2,16384]{2,1,0:T(2,128)(2,1)S(1)}, u32[]{:S(2)}, u32[]{:S(2)}) async-start(bf16[16,2,16384]{2,1,0:T(2,128)(2,1)} %reshape.191), calls=%async_computation | async-start | bytes 2097152 | tf_op jit(solution)/shard_map/all_to_all | solution.py:44
  38.3 34.3 %all-to-all-done = bf16[16,2,16384]{2,1,0:T(2,128)(2,1)S(1)} async-done(((bf16[16,2,16384]{2,1,0:T(2,128)(2,1)}), bf16[16,2,16384]{2,1,0:T(2,128)(2,1)S(1)}, u32[]{:S(2)}, u32[]{:S(2)}) %all-to-all-start) | async-done | bytes 1048608 | tf_op jit(solution)/shard_map/all_to_all | solution.py:44
  72.5 3.5 reshape.192
  76.0 1.8 copy.61
  77.8 3.2 fusion.130
  81.0 1.9 fusion.30
  83.1 0.9 fusion.131
  84.0 1.4 fusion.39
  85.5 0.6 fusion.132
  86.1 0.7 fusion.52
  87.6 2.3 fusion.65
  89.8 1.7 fusion.69
  91.6 1.1 convolution_convert_fusion.1
  92.7 0.6 convolution_convert_fusion.2
  93.3 0.7 pad_maximum_fusion.3
  94.3 1.3 fusion.137
  95.9 1.6 convolution_convert_fusion.4
  97.9 0.6 fusion.136
  98.5 1.0 fusion.59
  99.4 0.8 fusion.135
  100.3 1.3 fusion.41
  101.6 1.1 fusion.134
  102.7 1.8 fusion.32
  104.5 1.0 convolution_convert_fusion.3
  105.5 1.6 fusion.68
  107.1 2.2 fusion.64
  109.3 0.7 pad_maximum_fusion.2
  110.4 1.3 fusion.141
  111.9 1.5 fusion.140
  114.4 0.8 fusion.139
  115.2 1.2 fusion.45
  116.4 1.0 fusion.138
  117.4 0.9 convolution_convert_fusion
  118.3 1.8 fusion.33
  120.1 1.4 fusion.67
  121.4 2.0 fusion.63
  123.5 0.7 pad_maximum_fusion.1
  124.6 1.2 fusion.145
  125.9 1.4 fusion.144
  128.1 0.7 fusion.143
  128.8 1.1 fusion.48
  129.9 1.0 fusion.142
  130.9 0.7 convolution_convert_fusion.6
  131.6 1.6 fusion.35
  133.3 1.3 fusion.66
  134.6 1.9 fusion.70
  136.5 0.7 pad_maximum_fusion
  137.3 4.7 %all-gather.14.cloned.1.call-done = bf16[1024,2048]{1,0:T(8,128)(2,1)} async-done(((bf16[1024,128]{1,0:T(8,128)(2,1)}), bf16[1024,2048]{1,0:T(8,128)(2,1)}) %all-gather.14.cloned.1.call-update) | async-done | bytes 4194320 | tf_op jit(solution)/shard_map/all_gather | solution.py:70
  142.0 5.9 %fusion.149 = f32[1024,512]{1,0:T(8,128)} fusion(bf16[1024,2048]{1,0:T(8,128)(2,1)} %all-gather.14.cloned.1.call-done, bf16[2048,512]{1,0:T(8,128)(2,1)S(1)} %copy-done), kind=kOutput, calls=%fused_computation.289 | convolution fusion | flops 2147483648 | bytes 8388608 | tf_op jit(solution)/shard_map/dot_general | solution.py:71
  147.9 43.5 %all-gather.12.cloned.1.call-done = bf16[1024,2048]{1,0:T(8,128)(2,1)} async-done(((bf16[1024,128]{1,0:T(8,128)(2,1)}), bf16[1024,2048]{1,0:T(8,128)(2,1)}) %all-gather.12.cloned.1.call-update) | async-done | bytes 4194320 | tf_op jit(solution)/shard_map/all_gather | solution.py:70
  191.5 5.9 %fusion.148 = f32[1024,512]{1,0:T(8,128)} fusion(bf16[1024,2048]{1,0:T(8,128)(2,1)} %all-gather.12.cloned.1.call-done, bf16[2048,512]{1,0:T(8,128)(2,1)S(1)} %copy-done), kind=kOutput, calls=%fused_computation.288 | convolution fusion | flops 2147483648 | bytes 8388608 | tf_op jit(solution)/shard_map/dot_general | solution.py:71
  197.7 43.0 %all-gather.10.cloned.1.call-done = bf16[1024,2048]{1,0:T(8,128)(2,1)} async-done(((bf16[1024,128]{1,0:T(8,128)(2,1)}), bf16[1024,2048]{1,0:T(8,128)(2,1)}) %all-gather.10.cloned.1.call-update) | async-done | bytes 4194320 | tf_op jit(solution)/shard_map/all_gather | solution.py:70
  240.7 5.8 %fusion.147 = f32[1024,512]{1,0:T(8,128)} fusion(bf16[1024,2048]{1,0:T(8,128)(2,1)} %all-gather.10.cloned.1.call-done, bf16[2048,512]{1,0:T(8,128)(2,1)S(1)} %copy-done), kind=kOutput, calls=%fused_computation.287 | convolution fusion | flops 2147483648 | bytes 8388608 | tf_op jit(solution)/shard_map/dot_general | solution.py:71
  246.6 43.3 %all-gather.8.cloned.1.call-done = bf16[1024,2048]{1,0:T(8,128)(2,1)} async-done(((bf16[1024,128]{1,0:T(8,128)(2,1)}), bf16[1024,2048]{1,0:T(8,128)(2,1)}) %all-gather.8.cloned.1.call-update) | async-done | bytes 4194320 | tf_op jit(solution)/shard_map/all_gather | solution.py:70
  289.9 5.8 %fusion.146 = f32[1024,512]{1,0:T(8,128)} fusion(bf16[1024,2048]{1,0:T(8,128)(2,1)} %all-gather.8.cloned.1.call-done, bf16[2048,512]{1,0:T(8,128)(2,1)S(1)} %copy-done), kind=kOutput, calls=%fused_computation.286 | convolution fusion | flops 2147483648 | bytes 8388608 | tf_op jit(solution)/shard_map/dot_general | solution.py:71
  295.8 26.6 %reduce-scatter.11.cloned.1.call-done = f32[256,512]{1,0:T(8,128)} async-done(((f32[1024,512]{1,0:T(8,128)}), f32[256,512]{1,0:T(8,128)}) %reduce-scatter.11.cloned.1.call-update) | async-done | bytes 524304 | tf_op jit(solution)/shard_map/reduce_scatter | solution.py:72
  322.4 34.6 %reduce-scatter.9.cloned.1.call-done = f32[256,512]{1,0:T(8,128)} async-done(((f32[1024,512]{1,0:T(8,128)}), f32[256,512]{1,0:T(8,128)}) %reduce-scatter.9.cloned.1.call-update) | async-done | bytes 524304 | tf_op jit(solution)/shard_map/reduce_scatter | solution.py:72
  357.0 34.6 %reduce-scatter.7.cloned.1.call-done = f32[256,512]{1,0:T(8,128)} async-done(((f32[1024,512]{1,0:T(8,128)}), f32[256,512]{1,0:T(8,128)}) %reduce-scatter.7.cloned.1.call-update) | async-done | bytes 524304 | tf_op jit(solution)/shard_map/reduce_scatter | solution.py:72
  391.6 34.6 %reduce-scatter.5.cloned.1.call-done = f32[256,512]{1,0:T(8,128)} async-done(((f32[1024,512]{1,0:T(8,128)}), f32[256,512]{1,0:T(8,128)}) %reduce-scatter.5.cloned.1.call-update) | async-done | bytes 524304 | tf_op jit(solution)/shard_map/reduce_scatter | solution.py:72
  426.2 2.8 fusion.36
  (69 shorter events, 6.2 us)
Async XLA Ops:
  6.5 135.5 %copy-start = (bf16[2048,512]{1,0:T(8,128)(2,1)S(1)}, bf16[2048,512]{1,0:T(8,128)(2,1)}, u32[]{:S(2)}) copy-start(bf16[2048,512]{1,0:T(8,128)(2,1)} %param.7) | copy-start | bytes 6291460
  6.5 71.3 %all-gather.6.cloned.1.call-start = ((), (), s32[]{:S(2)}) async-start(), calls=%async_computation.5 | async-start | bytes 4456448 | tf_op jit(solution)/shard_map/all_gather | solution.py:48
  26.5 11.7 %copy-start.1 = (s32[4096]{0:T(1024)S(1)}, s32[4096]{0:T(1024)}, u32[]{:S(2)}) copy-start(s32[4096]{0:T(1024)} %param.9) | copy-start | bytes 49156
  27.6 44.9 %all-to-all-start = ((bf16[16,2,16384]{2,1,0:T(2,128)(2,1)}), bf16[16,2,16384]{2,1,0:T(2,128)(2,1)S(1)}, u32[]{:S(2)}, u32[]{:S(2)}) async-start(bf16[16,2,16384]{2,1,0:T(2,128)(2,1)} %reshape.191), calls=%async_computation | async-start | bytes 2097152 | tf_op jit(solution)/shard_map/all_to_all | solution.py:44
  37.6 104.4 %all-gather.14.cloned.1.call-start = ((), (), s32[]{:S(2)}) async-start(), calls=%async_computation.12 | async-start | bytes 4456448 | tf_op jit(solution)/shard_map/all_gather | solution.py:70
  81.0 2.2 copy-start.3
  94.0 97.5 %all-gather.12.cloned.1.call-start = ((), (), s32[]{:S(2)}) async-start(), calls=%async_computation.10 | async-start | bytes 4456448 | tf_op jit(solution)/shard_map/all_gather | solution.py:70
  95.6 2.3 copy-start.4
  110.0 130.7 %all-gather.10.cloned.1.call-start = ((), (), s32[]{:S(2)}) async-start(), calls=%async_computation.8 | async-start | bytes 4456448 | tf_op jit(solution)/shard_map/all_gather | solution.py:70
  110.4 3.6 copy-start.5
  124.2 165.7 %all-gather.8.cloned.1.call-start = ((), (), s32[]{:S(2)}) async-start(), calls=%async_computation.6 | async-start | bytes 4456448 | tf_op jit(solution)/shard_map/all_gather | solution.py:70
  124.5 3.2 copy-start.6
  137.2 185.1 %reduce-scatter.11.cloned.1.call-start = ((), (), s32[]{:S(2)}) async-start(), calls=%async_computation.13 | async-start | bytes 2621440 | tf_op jit(solution)/shard_map/reduce_scatter | solution.py:72
  147.9 209.1 %reduce-scatter.9.cloned.1.call-start = ((), (), s32[]{:S(2)}) async-start(), calls=%async_computation.11 | async-start | bytes 2621440 | tf_op jit(solution)/shard_map/reduce_scatter | solution.py:72
  197.4 194.2 %reduce-scatter.7.cloned.1.call-start = ((), (), s32[]{:S(2)}) async-start(), calls=%async_computation.9 | async-start | bytes 2621440 | tf_op jit(solution)/shard_map/reduce_scatter | solution.py:72
  246.6 179.6 %copy-start.2 = (bf16[1024,512]{1,0:T(8,128)(2,1)S(1)}, bf16[1024,512]{1,0:T(8,128)(2,1)}, u32[]{:S(2)}) copy-start(bf16[1024,512]{1,0:T(8,128)(2,1)} %param.8) | copy-start | bytes 3145732
  246.6 179.6 %reduce-scatter.5.cloned.1.call-start = ((), (), s32[]{:S(2)}) async-start(), calls=%async_computation.7 | async-start | bytes 2621440 | tf_op jit(solution)/shard_map/reduce_scatter | solution.py:72
Sparse Core Ops, SparseCore 0:
  9.2 64.9 all-gather.5
  94.2 47.7 all-gather.13
  143.8 47.6 all-gather.11
  193.1 47.5 all-gather.9
  242.3 47.5 all-gather.7
  292.3 30.0 reduce-scatter.10
  324.9 31.9 reduce-scatter.8
  359.5 31.9 reduce-scatter.6
  394.1 32.0 reduce-scatter.4
where the time goes:
time: 440 us; the launch traced here: 436 us
  waiting for transfers between devices  299 us (68%)
  matrix products  62.2 us (14%)
  other arithmetic  33.2 us (8%)
  local copies, waits for them, and re-layouts  15.3 us (3%)
  between operations  14.2 us (3%)
  starting transfers between devices  11.8 us (3%)
    all_gather x4, waiting for transfers between devices, on_device(): gathered = lax.all_gather(chunk_heads, 'seq', axis=1, tiled=True)  135 us
    reduce_scatter x4, waiting for transfers between devices, on_device(): lax.psum_scatter(projected, 'tensor', scatter_dimension=0, tiled=True)  130 us
    all_to_all x1, waiting for transfers between devices, on_device(): lax.all_to_all(query_slab, 'seq', split_axis=2, concat_axis=0, tiled=True)  34.3 us
    dot_general x4, matrix products, on_device(): jnp.dot(gathered, out_weight, preferred_element_type=jnp.float32)  23.4 us
    dot_general x16, matrix products, attend_rows(): jnp.einsum('qk,kd->qd', weights, value_head[:key_end], preferred_element_...  21 us
    dot_general x16, matrix products, attend_rows(): jnp.einsum('qd,kd->qk', query_block, key_head[:key_end], preferred_elemen...  17.8 us
    reduce_sum x16, other arithmetic, attend_rows(): jnp.sum(exponents, axis=-1, keepdims=True)  15.8 us
    unnamed x1, other arithmetic  11.6 us
  transfers between devices with their start and end apart: 10, of which 9 were waited for; matrix products, arithmetic and copies ran while one was open for 21% of the time, Pallas kernels for 0%

commit v1 on v0

--- a/solution.py
+++ b/solution.py
@@ -9,6 +9,12 @@
 HD = 128
 L = 4096
 CHUNKS = 4
+
+
+def trace_shapes(obj, which_axis):
+    return jnp.concatenate(
+        lax.all_to_all(jnp.stack(lax.axis_size(which_axis) * [obj]), which_axis, 0, 0), 1
+    )
 
 
 def attend_rows(query_head, key_head, value_head, doc_ids, first_row, rows):
@@ -67,7 +73,7 @@
             for part in range(n_ten)
         ]
         chunk_heads = jnp.concatenate(blocks, axis=0)
-        gathered = lax.all_gather(chunk_heads, "seq", axis=1, tiled=True)
+        gathered = trace_shapes(chunk_heads, "seq")
         projected = jnp.dot(gathered, out_weight, preferred_element_type=jnp.float32)
         pieces.append(lax.psum_scatter(projected, "tensor", scatter_dimension=0, tiled=True))
     summed = jnp.concatenate(pieces, axis=0)

time: 440 us -> 549 us (1.25)
  waiting for transfers between devices: 299 us -> 372 us
  starting transfers between devices: 11.8 us -> 33.1 us
  local copies, waits for them, and re-layouts: 15.3 us -> 29.1 us
    all_to_all x0 -> x4, waiting for transfers between devices: none -> 306 us  [trace_shapes(): lax.all_to_all(jnp.stack(lax.axis_size(which_axis) * [obj]), which_axis,...]
    all_gather x4 -> x0, waiting for transfers between devices: 135 us -> none  [on_device(): gathered = lax.all_gather(chunk_heads, 'seq', axis=1, tiled=True)]
    reduce_scatter x4, waiting for transfers between devices: 130 us -> 31.6 us  [on_device(): lax.psum_scatter(projected, 'tensor', scatter_dimension=0, tiled=True)]
    all_to_all x0 -> x4, starting transfers between devices: none -> 22 us  [trace_shapes(): lax.all_to_all(jnp.stack(lax.axis_size(which_axis) * [obj]), which_axis,...]
    another operation x0 -> x4, local copies, waits for them, and re-layouts: none -> 9.96 us  [trace_shapes(): jnp.stack(lax.axis_size(which_axis) * [obj])]
  transfers between devices with their start and end apart: 10 -> 10, of which waited for: 9 -> 6; matrix products, arithmetic and copies ran while one was open for 21% -> 18% of each run, Pallas kernels for 0% -> 0%
where the time goes in v1:
time: 549 us; the launch traced here: 546 us
  waiting for transfers between devices  372 us (68%)
  matrix products  65.2 us (12%)
  starting transfers between devices  33.1 us (6%)
  other arithmetic  32.5 us (6%)
  local copies, waits for them, and re-layouts  29.1 us (5%)
  between operations  13.9 us (3%)
    all_to_all x4, waiting for transfers between devices, trace_shapes(): lax.all_to_all(jnp.stack(lax.axis_size(which_axis) * [obj]), which_axis,...  306 us
    all_to_all x1, waiting for transfers between devices, on_device(): lax.all_to_all(query_slab, 'seq', split_axis=2, concat_axis=0, tiled=True)  34.2 us
    reduce_scatter x4, waiting for transfers between devices, on_device(): lax.psum_scatter(projected, 'tensor', scatter_dimension=0, tiled=True)  31.6 us
    dot_general x4, matrix products, on_device(): jnp.dot(gathered, out_weight, preferred_element_type=jnp.float32)  23.6 us
    all_to_all x4, starting transfers between devices, trace_shapes(): lax.all_to_all(jnp.stack(lax.axis_size(which_axis) * [obj]), which_axis,...  22 us
    dot_general x16, matrix products, attend_rows(): jnp.einsum('qk,kd->qd', weights, value_head[:key_end], preferred_element_...  21.3 us
    dot_general x16, matrix products, attend_rows(): jnp.einsum('qd,kd->qk', query_block, key_head[:key_end], preferred_elemen...  20.3 us
    reduce_sum x16, other arithmetic, attend_rows(): jnp.sum(exponents, axis=-1, keepdims=True)  15.8 us
  transfers between devices with their start and end apart: 10, of which 6 were waited for; matrix products, arithmetic and copies ran while one was open for 18% of the time, Pallas kernels for 0%

profile of v1, /device:TPU:1, one launch (start us, length us, event | category | flops | bytes accessed | tf_op | source)
XLA Modules:
  0.0 545.5 jit_solution(14238716878264238421)
XLA Ops:
  6.5 1.8 copy.55
  8.4 5.9 %copy.56 = bf16[256,1,2048]{0,1,2:T(2,128)(2,1)} copy(bf16[256,1,2048]{2,0,1:T(8,128)(2,1)} %bitcast.328) | data formatting | bytes 2097152 | tf_op jit(solution)/shard_map/reshape | solution.py:49
  14.8 11.6 %reduce = bf16[2048,256]{1,0:T(8,128)(2,1)S(1)} reduce(bf16[2048,1,256]{2,1,0:T(2,128)(2,1)} %bitcast.318, bf16[]{:T(256)} %broadcast.180), dimensions={1}, to_apply=%bitcast.240.reduce_sub_computation | reduce | bytes 2097154
  26.5 1.1 reshape.231
  27.6 10.6 %all-to-all-start = ((bf16[16,2,16384]{2,1,0:T(2,128)(2,1)}), bf16[16,2,16384]{2,1,0:T(2,128)(2,1)S(1)}, u32[]{:S(2)}, u32[]{:S(2)}) async-start(bf16[16,2,16384]{2,1,0:T(2,128)(2,1)} %reshape.231), calls=%async_computation | async-start | bytes 2097152 | tf_op jit(solution)/shard_map/all_to_all | solution.py:50
  38.3 34.2 %all-to-all-done = bf16[16,2,16384]{2,1,0:T(2,128)(2,1)S(1)} async-done(((bf16[16,2,16384]{2,1,0:T(2,128)(2,1)}), bf16[16,2,16384]{2,1,0:T(2,128)(2,1)S(1)}, u32[]{:S(2)}, u32[]{:S(2)}) %all-to-all-start) | async-done | bytes 1048608 | tf_op jit(solution)/shard_map/all_to_all | solution.py:50
  72.5 3.5 reshape.232
  76.0 1.8 copy.77
  77.8 1.3 fusion.141
  79.3 1.5 fusion.140
  82.1 1.2 fusion.45
  83.4 1.0 fusion.138
  84.4 1.7 fusion.33
  86.6 0.9 convolution_convert_fusion
  87.5 1.4 fusion.67
  88.9 2.0 fusion.63
  91.6 1.1 copy.66
  92.7 2.5 stack.9
  95.2 4.9 all-to-all-start.2
  100.2 1.2 fusion.145
  101.5 1.4 fusion.144
  104.4 1.1 fusion.48
  105.6 1.0 fusion.142
  107.3 1.7 fusion.35
  108.9 1.3 fusion.66
  110.2 1.9 fusion.70
  112.8 1.1 copy.61
  113.9 79.6 %all-to-all-done.2 = bf16[16,1024,128]{1,2,0:T(8,128)(2,1)} async-done(((bf16[16,1024,128]{1,2,0:T(8,128)(2,1)}), bf16[16,1024,128]{1,2,0:T(8,128)(2,1)}, u32[]{:S(2)}, u32[]{:S(2)}) %all-to-all-start.2) | async-done | bytes 4194336 | tf_op jit(solution)/shard_map/all_to_all | solution.py:16
  193.5 2.5 stack.8
  196.0 5.9 %all-to-all-start.1 = ((bf16[16,1024,128]{1,2,0:T(8,128)(2,1)}), bf16[16,1024,128]{1,2,0:T(8,128)(2,1)}, u32[]{:S(2)}, u32[]{:S(2)}) async-start(bf16[16,1024,128]{1,2,0:T(8,128)(2,1)} %stack.8), calls=%async_computation.1 | async-start | bytes 8388608 | tf_op jit(solution)/shard_map/all_to_all | solution.py:16
  201.9 1.4 fusion.133
  203.6 1.9 fusion.132
  206.9 0.9 fusion.131
  207.8 1.2 fusion.130
  209.0 1.4 fusion.39
  210.4 1.9 fusion.30
  212.4 1.1 convolution_convert_fusion.1
  213.5 1.7 fusion.69
  215.2 2.3 fusion.65
  218.3 1.1 copy.76
  219.4 75.9 %all-to-all-done.1 = bf16[16,1024,128]{1,2,0:T(8,128)(2,1)} async-done(((bf16[16,1024,128]{1,2,0:T(8,128)(2,1)}), bf16[16,1024,128]{1,2,0:T(8,128)(2,1)}, u32[]{:S(2)}, u32[]{:S(2)}) %all-to-all-start.1) | async-done | bytes 4194336 | tf_op jit(solution)/shard_map/all_to_all | solution.py:16
  295.2 2.5 stack.11
  297.7 5.5 %all-to-all-start.4 = ((bf16[16,1024,128]{1,2,0:T(8,128)(2,1)}), bf16[16,1024,128]{1,2,0:T(8,128)(2,1)}, u32[]{:S(2)}, u32[]{:S(2)}) async-start(bf16[16,1024,128]{1,2,0:T(8,128)(2,1)} %stack.11), calls=%async_computation.7 | async-start | bytes 8388608 | tf_op jit(solution)/shard_map/all_to_all | solution.py:16
  303.7 1.3 fusion.137
  305.0 0.9 copy-done.4
  306.1 2.8 fusion.136
  308.9 5.9 %fusion.147 = f32[1024,512]{1,0:T(8,128)} fusion(bf16[1024,2048]{0,1:T(8,128)(2,1)} %bitcast.37, bf16[2048,512]{1,0:T(8,128)(2,1)S(1)} %copy-done), kind=kOutput, calls=%fused_computation.287 | convolution fusion | flops 2147483648 | bytes 8388608 | tf_op jit(solution)/shard_map/dot_general | solution.py:77
  314.9 1.8 convolution_convert_fusion.4
  316.7 1.0 fusion.59
  318.7 1.3 fusion.41
  320.1 1.1 fusion.134
  321.1 1.8 fusion.32
  323.0 1.0 convolution_convert_fusion.3
  324.0 1.5 fusion.68
  325.5 2.2 fusion.64
  327.9 68.8 %all-to-all-done.4 = bf16[16,1024,128]{1,2,0:T(8,128)(2,1)} async-done(((bf16[16,1024,128]{1,2,0:T(8,128)(2,1)}), bf16[16,1024,128]{1,2,0:T(8,128)(2,1)}, u32[]{:S(2)}, u32[]{:S(2)}) %all-to-all-start.4) | async-done | bytes 4194336 | tf_op jit(solution)/shard_map/all_to_all | solution.py:16
  396.7 2.5 stack.10
  399.2 5.7 %all-to-all-start.3 = ((bf16[16,1024,128]{1,2,0:T(8,128)(2,1)}), bf16[16,1024,128]{1,2,0:T(8,128)(2,1)}, u32[]{:S(2)}, u32[]{:S(2)}) async-start(bf16[16,1024,128]{1,2,0:T(8,128)(2,1)} %stack.10), calls=%async_computation.5 | async-start | bytes 8388608 | tf_op jit(solution)/shard_map/all_to_all | solution.py:16
  404.9 5.9 %fusion.146 = f32[1024,512]{1,0:T(8,128)} fusion(bf16[1024,2048]{0,1:T(8,128)(2,1)} %bitcast.19, bf16[2048,512]{1,0:T(8,128)(2,1)S(1)} %copy-done), kind=kOutput, calls=%fused_computation.286 | convolution fusion | flops 2147483648 | bytes 8388608 | tf_op jit(solution)/shard_map/dot_general | solution.py:77
  410.9 5.9 %fusion.149 = f32[1024,512]{1,0:T(8,128)} fusion(bf16[1024,2048]{0,1:T(8,128)(2,1)} %bitcast.73, bf16[2048,512]{1,0:T(8,128)(2,1)S(1)} %copy-done), kind=kOutput, calls=%fused_computation.289 | convolution fusion | flops 2147483648 | bytes 8388608 | tf_op jit(solution)/shard_map/dot_general | solution.py:77
  416.8 81.6 %all-to-all-done.3 = bf16[16,1024,128]{1,2,0:T(8,128)(2,1)} async-done(((bf16[16,1024,128]{1,2,0:T(8,128)(2,1)}), bf16[16,1024,128]{1,2,0:T(8,128)(2,1)}, u32[]{:S(2)}, u32[]{:S(2)}) %all-to-all-start.3) | async-done | bytes 4194336 | tf_op jit(solution)/shard_map/all_to_all | solution.py:16
  498.4 6.0 %fusion.148 = f32[1024,512]{1,0:T(8,128)} fusion(bf16[1024,2048]{0,1:T(8,128)(2,1)} %bitcast.55, bf16[2048,512]{1,0:T(8,128)(2,1)S(1)} %copy-done), kind=kOutput, calls=%fused_computation.288 | convolution fusion | flops 2147483648 | bytes 8388608 | tf_op jit(solution)/shard_map/dot_general | solution.py:77
  504.5 31.5 %reduce-scatter.9.cloned.1.call-done = f32[256,512]{1,0:T(8,128)} async-done(((f32[1024,512]{1,0:T(8,128)}), f32[256,512]{1,0:T(8,128)}) %reduce-scatter.9.cloned.1.call-update) | async-done | bytes 524304 | tf_op jit(solution)/shard_map/reduce_scatter | solution.py:78
  536.0 2.8 fusion.36
  (77 shorter events, 10.8 us)
Async XLA Ops:
  6.5 302.4 %copy-start = (bf16[2048,512]{1,0:T(8,128)(2,1)S(1)}, bf16[2048,512]{1,0:T(8,128)(2,1)}, u32[]{:S(2)}) copy-start(bf16[2048,512]{1,0:T(8,128)(2,1)} %param.7) | copy-start | bytes 6291460
  6.5 71.3 %all-gather.2.cloned.1.call-start = ((), (), s32[]{:S(2)}) async-start(), calls=%async_computation.9 | async-start | bytes 4456448 | tf_op jit(solution)/shard_map/all_gather | solution.py:54
  26.5 11.7 %copy-start.1 = (s32[4096]{0:T(1024)S(1)}, s32[4096]{0:T(1024)}, u32[]{:S(2)}) copy-start(s32[4096]{0:T(1024)} %param.9) | copy-start | bytes 49156
  27.6 44.9 %all-to-all-start = ((bf16[16,2,16384]{2,1,0:T(2,128)(2,1)}), bf16[16,2,16384]{2,1,0:T(2,128)(2,1)S(1)}, u32[]{:S(2)}, u32[]{:S(2)}) async-start(bf16[16,2,16384]{2,1,0:T(2,128)(2,1)} %reshape.231), calls=%async_computation | async-start | bytes 2097152 | tf_op jit(solution)/shard_map/all_to_all | solution.py:50
  77.8 3.6 copy-start.5
  95.2 98.3 %all-to-all-start.2 = ((bf16[16,1024,128]{1,2,0:T(8,128)(2,1)}), bf16[16,1024,128]{1,2,0:T(8,128)(2,1)}, u32[]{:S(2)}, u32[]{:S(2)}) async-start(bf16[16,1024,128]{1,2,0:T(8,128)(2,1)} %stack.9), calls=%async_computation.3 | async-start | bytes 8388608 | tf_op jit(solution)/shard_map/all_to_all | solution.py:16
  100.1 3.3 copy-start.6
  196.0 99.2 %all-to-all-start.1 = ((bf16[16,1024,128]{1,2,0:T(8,128)(2,1)}), bf16[16,1024,128]{1,2,0:T(8,128)(2,1)}, u32[]{:S(2)}, u32[]{:S(2)}) async-start(bf16[16,1024,128]{1,2,0:T(8,128)(2,1)} %stack.8), calls=%async_computation.1 | async-start | bytes 8388608 | tf_op jit(solution)/shard_map/all_to_all | solution.py:16
  203.6 2.6 copy-start.7
  297.7 99.0 %all-to-all-start.4 = ((bf16[16,1024,128]{1,2,0:T(8,128)(2,1)}), bf16[16,1024,128]{1,2,0:T(8,128)(2,1)}, u32[]{:S(2)}, u32[]{:S(2)}) async-start(bf16[16,1024,128]{1,2,0:T(8,128)(2,1)} %stack.11), calls=%async_computation.7 | async-start | bytes 8388608 | tf_op jit(solution)/shard_map/all_to_all | solution.py:16
  303.2 201.2 %reduce-scatter.7.cloned.1.call-start = ((), (), s32[]{:S(2)}) async-start(), calls=%async_computation.11 | async-start | bytes 2621440 | tf_op jit(solution)/shard_map/reduce_scatter | solution.py:78
  305.0 0.9 copy-start.4
  314.9 1.9 copy-start.2
  314.9 3.0 copy-start.8
  399.2 99.2 %all-to-all-start.3 = ((bf16[16,1024,128]{1,2,0:T(8,128)(2,1)}), bf16[16,1024,128]{1,2,0:T(8,128)(2,1)}, u32[]{:S(2)}, u32[]{:S(2)}) async-start(bf16[16,1024,128]{1,2,0:T(8,128)(2,1)} %stack.10), calls=%async_computation.5 | async-start | bytes 8388608 | tf_op jit(solution)/shard_map/all_to_all | solution.py:16
  404.9 99.6 %reduce-scatter.5.cloned.1.call-start = ((), (), s32[]{:S(2)}) async-start(), calls=%async_computation.10 | async-start | bytes 2621440 | tf_op jit(solution)/shard_map/reduce_scatter | solution.py:78
  410.8 93.6 %reduce-scatter.11.cloned.1.call-start = ((), (), s32[]{:S(2)}) async-start(), calls=%async_computation.13 | async-start | bytes 2621440 | tf_op jit(solution)/shard_map/reduce_scatter | solution.py:78
  416.8 119.2 %reduce-scatter.9.cloned.1.call-start = ((), (), s32[]{:S(2)}) async-start(), calls=%async_computation.12 | async-start | bytes 2621440 | tf_op jit(solution)/shard_map/reduce_scatter | solution.py:78
  498.4 37.6 %copy-start.3 = (bf16[1024,512]{1,0:T(8,128)(2,1)S(1)}, bf16[1024,512]{1,0:T(8,128)(2,1)}, u32[]{:S(2)}) copy-start(bf16[1024,512]{1,0:T(8,128)(2,1)} %param.8) | copy-start | bytes 3145732
Sparse Core Ops, SparseCore 0:
  9.2 64.9 all-gather.1
  315.0 33.1 reduce-scatter.6
  411.0 33.1 reduce-scatter.4
  446.6 32.0 reduce-scatter.10
  504.5 31.4 reduce-scatter.8
